TPU v7x, 128 devices: a whole 4x4x4 slice. The times are simulated.
128 devices in a mesh: dp: 8 (over z, core), seq: 16 (over y, x).
Axes of the slice: x: 4, y: 4, z: 4, core: 2. Of those that a mesh axis runs over, the one named last changes fastest.
Arguments:
- tokens: bfloat16 [8, 8192, 2048], P('dp', 'seq'), may hold values from -6 to 6
- input_gain: bfloat16 [2048], replicated, may hold values from 0.099609375 to 1.8984375
- qkv_weight: bfloat16 [2048, 6144], P(None, ('dp', 'seq')), may hold values from -0.125 to 0.125
- head_gain: bfloat16 [2048], replicated, may hold values from 0.099609375 to 1.8984375
- prefix_state: float32 [8, 16, 128, 128], P('dp'), may hold values from -256 to 256
Outputs:
- attended: bfloat16 [8, 8192, 2048], P('dp', 'seq')
All inputs are finite; a program needn't handle non-finite values.
Results may differ from a plain program's by a relative error of at most 0.0061.
Values may be sent and summed in bfloat16 or wider, within the bound.
No kernel may reach another device: no remote copies, remote signals or barrier semaphores. Data moves between devices by JAX's collectives and lax.ppermute only.
A program may use at most 128 MiB of HBM per device.

v0:
```python
import jax
import jax.numpy as jnp
from jax import lax
from jax.sharding import PartitionSpec as P

D = 2048
H = 16
DH = 128
BLOCK = 512
epsilon = 1e-05


def feature_map(inputs):
    return jnp.where(inputs > 0, inputs + 1.0, jnp.exp(jnp.minimum(inputs, 0.0)))


def span_attention(queries, key_feats, values, memory, head_gain):
    num_blocks = queries.shape[0] // BLOCK
    causal = jnp.arange(BLOCK)[:, None] >= jnp.arange(BLOCK)[None, :]
    gains = head_gain.astype(jnp.float32).reshape(H, DH)

    def advance(running, blocks):
        query_blk, key_blk, value_blk = blocks
        carried = jnp.einsum(
            "bhd,hde->bhe",
            query_blk,
            running.astype(jnp.bfloat16),
            preferred_element_type=jnp.float32,
        )
        scores = jnp.einsum("bhd,chd->hbc", query_blk, key_blk, preferred_element_type=jnp.float32)
        scores = jnp.where(causal[None], scores, 0.0).astype(jnp.bfloat16)
        within = jnp.einsum("hbc,che->bhe", scores, value_blk, preferred_element_type=jnp.float32)
        numerator = carried + within
        scale = lax.rsqrt(jnp.mean(numerator * numerator, axis=-1, keepdims=True) + epsilon)
        running = running + jnp.einsum(
            "bhd,bhe->hde", key_blk, value_blk, preferred_element_type=jnp.float32
        )
        return (running, (numerator * scale * gains).astype(jnp.bfloat16))

    def shaped(inputs):
        return inputs.reshape(num_blocks, BLOCK, H, DH)

    final_memory, outputs = lax.scan(
        advance, memory, (shaped(queries), shaped(key_feats), shaped(values))
    )
    return outputs.reshape(num_blocks * BLOCK, H * DH)


def body(tokens, input_gain, qkv_weight, head_gain, prefix_state):
    inputs = tokens[0].astype(jnp.float32)
    normed = inputs * lax.rsqrt(jnp.mean(inputs * inputs, axis=-1, keepdims=True) + epsilon)
    normed = (normed * input_gain.astype(jnp.float32)).astype(jnp.bfloat16)
    tok_rows = normed.shape[0]
    projected = jnp.dot(
        normed,
        lax.all_gather(qkv_weight, ("dp", "seq"), axis=1, tiled=True),
        preferred_element_type=jnp.float32,
    )
    queries = feature_map(projected[:, :D]).astype(jnp.bfloat16).reshape(tok_rows, H, DH)
    key_feats = feature_map(projected[:, D : 2 * D]).astype(jnp.bfloat16).reshape(tok_rows, H, DH)
    values = projected[:, 2 * D :].astype(jnp.bfloat16).reshape(tok_rows, H, DH)
    local = jnp.einsum(
        "thd,the->hde", key_feats, values, preferred_element_type=jnp.float32
    ).astype(jnp.bfloat16)
    gathered = lax.all_gather(local[None], "seq", axis=0, tiled=True)
    my_index = lax.axis_index("seq")
    earlier = (jnp.arange(gathered.shape[0]) < my_index).astype(jnp.bfloat16)
    before = jnp.einsum("c,chde->hde", earlier, gathered, preferred_element_type=jnp.float32)
    memory = prefix_state[0] + before
    attended = span_attention(queries, key_feats, values, memory, head_gain)
    return attended[None]


def solution(mesh):
    placed = (P("dp", "seq", None), P(), P(None, ("dp", "seq")), P(), P("dp", None, None, None))
    return jax.shard_map(
        body, mesh=mesh, in_specs=placed, out_specs=P("dp", "seq", None), check_vma=False
    )
```

profile of v0, /device:TPU:1, one launch (start us, length us, event | category | flops | bytes accessed | tf_op | source)
XLA Modules:
  0.0 235.7 jit_solution(6228382882600847953)
XLA Ops:
  6.5 0.0 all-gather.4.cloned.1.call-start
  6.5 0.7 all-gather.4.cloned.1.call-update
  7.3 0.0 all-gather.6.cloned.1.call-start
  7.3 0.7 convert_element_type.38
  8.0 2.1 fusion.2
  10.1 97.0 %all-gather.4.cloned.1.call-done = bf16[2048,6144]{0,1:T(8,128)(2,1)} async-done(((bf16[2048,48]{0,1:T(8,128)(2,1)}), bf16[2048,6144]{0,1:T(8,128)(2,1)}) %all-gather.4.cloned.1.call-update) | async-done | bytes 25165840 | tf_op jit(solution)/shard_map/all_gather | solution.py:56
  107.1 20.0 %fusion.10 = f32[512,6144]{1,0:T(8,128)} fusion(bf16[2048,6144]{0,1:T(8,128)(2,1)} %all-gather.4.cloned.1.call-done, bf16[1,512,2048]{2,1,0:T(8,128)(2,1)} %param.5, f32[2048]{0:T(1024)S(1)} %convert_element_type.38, f32[512]{0:T(512)S(1)} %add_rsqrt_fusion.1), kind=kOutput, calls=%fused_computation.19 | convolution fusion | flops 12889096192 | bytes 39856128 | tf_op jit(solution)/shard_map/dot_general | solution.py:54
  127.1 5.7 %fusion.9 = (bf16[64,16,8,128]{3,2,1,0:T(8,128)(2,1)}, bf16[512,2048]{1,0:T(8,128)(2,1)}) fusion(f32[512,6144]{1,0:T(8,128)} %fusion.10), kind=kLoop, calls=%fused_computation.18 | loop fusion | flops 10485760 | bytes 12582912
  132.8 3.8 %slice.21 = bf16[512,2048]{1,0:T(8,128)(2,1)} slice(f32[512,6144]{1,0:T(8,128)} %fusion.10), slice={[0:512], [4096:6144]} | slice | bytes 4194304 | tf_op jit(solution)/shard_map/slice | solution.py:61
  136.6 2.9 %copy.22 = bf16[512,2048]{0,1:T(8,128)(2,1)S(1)} copy(bf16[512,2048]{1,0:T(8,128)(2,1)} %get-tuple-element.20) | data formatting | bytes 4194304 | tf_op jit(solution)/shard_map/reshape | solution.py:60
  139.5 0.0 copy-start.3
  139.5 4.0 %copy.23 = bf16[512,2048]{0,1:T(8,128)(2,1)} copy(bf16[512,2048]{1,0:T(8,128)(2,1)} %slice.21) | data formatting | bytes 4194304 | tf_op jit(solution)/shard_map/reshape | solution.py:61
  143.5 3.1 %convolution_convert_fusion = bf16[16,128,128]{2,1,0:T(8,128)(2,1)} fusion(bf16[512,16,128]{0,2,1:T(8,128)(2,1)S(1)} %bitcast.53, bf16[512,16,128]{0,2,1:T(8,128)(2,1)} %bitcast.55), kind=kOutput, calls=%fused_computation.27 | convolution fusion | flops 268697600 | bytes 4718592 | tf_op jit(solution)/shard_map/thd,the->hde/dot_general | solution.py:62
  146.6 0.0 all-gather.6.cloned.1.call-update
  146.6 0.1 iota_compare_fusion
  146.7 0.0 copy-done.3
  146.7 9.2 %fusion.8 = f32[16,128,512]{2,1,0:T(8,128)} fusion(bf16[512,16,128]{0,2,1:T(8,128)(2,1)} %bitcast.56, bf16[512,16,128]{0,2,1:T(8,128)(2,1)S(1)} %bitcast.54, pred[512,512]{1,0:T(8,128)(4,1)S(1)} %iota_compare_fusion, bf16[64,16,8,128]{3,2,1,0:T(8,128)(2,1)} %get-tuple-element.19), kind=kOutput, calls=%fused_computation.16 | convolution fusion | flops 2155872256 | bytes 10747904 | tf_op jit(solution)/shard_map/while/body/eval_jaxpr/hbc,che->bhe/dot_general | solution.py:32
  155.9 60.4 %all-gather.6.cloned.1.call-done = bf16[256,128,128]{2,1,0:T(8,128)(2,1)} async-done(((bf16[16,128,128]{2,1,0:T(8,128)(2,1)}), bf16[256,128,128]{2,1,0:T(8,128)(2,1)}) %all-gather.6.cloned.1.call-update) | async-done | bytes 8388624 | tf_op jit(solution)/shard_map/all_gather | solution.py:65
  216.3 0.0 copy-start
  216.3 0.0 copy-start.1
  216.3 0.0 copy-start.2
  216.3 8.4 %fusion = f32[1,16,128,128]{3,0,2,1:T(1,128)S(1)} fusion(bf16[16,16,128,128]{3,2,1,0:T(8,128)(2,1)} %bitcast.52, s32[]{:T(128)S(6)} %axis_index.12), kind=kOutput, calls=%fused_computation.1 | convolution fusion | flops 8388624 | bytes 9437188 | tf_op jit(solution)/shard_map/c,chde->hde/dot_general | solution.py:68
  224.8 0.0 copy-done
  224.8 0.0 copy-done.1
  224.8 0.0 copy-done.2
  224.8 1.0 fusion.5
  225.9 0.6 fusion.7
  226.5 2.4 %copy.17 = bf16[1,512,2048]{2,1,0:T(8,128)(2,1)} copy(bf16[1,512,2048]{1,2,0:T(8,128)(2,1)S(1)} %bitcast.57) | data formatting | bytes 4194304 | tf_op jit(solution)/shard_map/broadcast_in_dim;reshape | solution.py:71
  (3 shorter events, 0.0 us)
Async XLA Ops:
  6.5 100.6 %all-gather.4.cloned.1.call-start = ((), (), s32[]{:S(2)}) async-start(), calls=%async_computation | async-start | bytes 25362432 | tf_op jit(solution)/shard_map/all_gather | solution.py:56
  7.3 209.1 %all-gather.6.cloned.1.call-start = ((), (), s32[]{:S(2)}) async-start(), calls=%async_computation.1 | async-start | bytes 8912896 | tf_op jit(solution)/shard_map/all_gather | solution.py:65
  139.5 7.2 %copy-start.3 = (bf16[2048]{0:T(1024)(128)(2,1)S(1)}, bf16[2048]{0:T(1024)(128)(2,1)}, u32[]{:S(2)}) copy-start(bf16[2048]{0:T(1024)(128)(2,1)} %param.8) | copy-start | bytes 12292
  216.3 8.5 %copy-start = (bf16[64,16,8,128]{3,2,1,0:T(8,128)(2,1)S(1)}, bf16[64,16,8,128]{3,2,1,0:T(8,128)(2,1)}, u32[]{:S(2)}) copy-start(bf16[64,16,8,128]{3,2,1,0:T(8,128)(2,1)} %get-tuple-element.19) | copy-start | bytes 6291460
  216.3 8.5 %copy-start.1 = (f32[16,128,512]{2,1,0:T(8,128)S(1)}, f32[16,128,512]{2,1,0:T(8,128)}, u32[]{:S(2)}) copy-start(f32[16,128,512]{2,1,0:T(8,128)} %fusion.8) | copy-start | bytes 12582916
  216.3 8.5 %copy-start.2 = (f32[1,16,128,128]{3,2,1,0:T(8,128)S(1)}, f32[1,16,128,128]{3,2,1,0:T(8,128)}, u32[]{:S(2)}) copy-start(f32[1,16,128,128]{3,2,1,0:T(8,128)} %param.9) | copy-start | bytes 3145732
Sparse Core Ops, SparseCore 0:
  10.4 96.6 all-gather.3
  146.7 69.5 all-gather.5
where the time goes:
time: 236 us
  waiting for transfers between devices  158 us (67%)
  matrix products  41.8 us (18%)
  between operations  13.5 us (6%)
  local copies, waits for them, and re-layouts  13 us (6%)
  other arithmetic  9.23 us (4%)
    all_gather x1, waiting for transfers between devices, body(): lax.all_gather(qkv_weight, ('dp', 'seq'), axis=1, tiled=True)  97 us
    all_gather x1, waiting for transfers between devices, body(): gathered = lax.all_gather(local[None], 'seq', axis=0, tiled=True)  60.4 us
    dot_general x1, matrix products, body(): jnp.dot(normed, lax.all_gather(qkv_weight, ('dp', 'seq'), axis=1, tiled=T...  20 us
    dot_general x1, matrix products, advance(): jnp.einsum('hbc,che->bhe', scores, value_blk, preferred_element_type=jnp....  9.24 us
    dot_general x1, matrix products, body(): jnp.einsum('c,chde->hde', earlier, gathered, preferred_element_type=jnp.f...  8.45 us
    unnamed x1, other arithmetic  5.73 us
  transfers between devices with their start and end apart: 2, of which 2 were waited for; matrix products, arithmetic and copies ran while one was open for 5% of the time, Pallas kernels for 0%

commit v1 on v0

--- a/solution.py
+++ b/solution.py
@@ -8,6 +8,9 @@
 DH = 128
 BLOCK = 512
 epsilon = 1e-05
+map_row = lambda panel: jnp.concatenate(
+    lax.all_to_all(jnp.stack([panel for _ in range(lax.axis_size("seq"))]), "seq", 0, 0), axis=0
+)
 
 
 def feature_map(inputs):
@@ -62,7 +65,7 @@
     local = jnp.einsum(
         "thd,the->hde", key_feats, values, preferred_element_type=jnp.float32
     ).astype(jnp.bfloat16)
-    gathered = lax.all_gather(local[None], "seq", axis=0, tiled=True)
+    gathered = map_row(local[None])
     my_index = lax.axis_index("seq")
     earlier = (jnp.arange(gathered.shape[0]) < my_index).astype(jnp.bfloat16)
     before = jnp.einsum("c,chde->hde", earlier, gathered, preferred_element_type=jnp.float32)

time: 236 us -> 303 us (1.28)
  waiting for transfers between devices: 158 us -> 213 us
  starting transfers between devices: 0.04 us -> 6.73 us
  local copies, waits for them, and re-layouts: 13 us -> 18.5 us
    all_to_all x0 -> x1, waiting for transfers between devices: none -> 116 us  [lax.all_to_all(jnp.stack([panel for _ in range(lax.axis_size('seq'))]), '...]
    all_gather x1 -> x0, waiting for transfers between devices: 60.4 us -> none  [body(): gathered = lax.all_gather(local[None], 'seq', axis=0, tiled=True)]
    all_to_all x0 -> x1, starting transfers between devices: none -> 6.73 us  [lax.all_to_all(jnp.stack([panel for _ in range(lax.axis_size('seq'))]), '...]
    another operation x0 -> x1, local copies, waits for them, and re-layouts: none -> 5.43 us  [jnp.stack([panel for _ in range(lax.axis_size('seq'))])]
  transfers between devices with their start and end apart: 2 -> 2, of which waited for: 2 -> 2; matrix products, arithmetic and copies ran while one was open for 5% -> 4% of each run, Pallas kernels for 0% -> 0%
where the time goes in v1:
time: 303 us; the launch traced here: 302 us
  waiting for transfers between devices  213 us (70%)
  matrix products  40.9 us (13%)
  local copies, waits for them, and re-layouts  18.5 us (6%)
  between operations  13.5 us (4%)
  other arithmetic  9.25 us (3%)
  starting transfers between devices  6.73 us (2%)
    all_to_all x1, waiting for transfers between devices, lax.all_to_all(jnp.stack([panel for _ in range(lax.axis_size('seq'))]), '...  116 us
    all_gather x1, waiting for transfers between devices, body(): lax.all_gather(qkv_weight, ('dp', 'seq'), axis=1, tiled=True)  97.1 us
    dot_general x1, matrix products, body(): jnp.dot(normed, lax.all_gather(qkv_weight, ('dp', 'seq'), axis=1, tiled=T...  19.9 us
    dot_general x1, matrix products, advance(): jnp.einsum('hbc,che->bhe', scores, value_blk, preferred_element_type=jnp....  9.21 us
    dot_general x1, matrix products, body(): jnp.einsum('c,chde->hde', earlier, gathered, preferred_element_type=jnp.f...  8.45 us
    all_to_all x1, starting transfers between devices, lax.all_to_all(jnp.stack([panel for _ in range(lax.axis_size('seq'))]), '...  6.73 us
  transfers between devices with their start and end apart: 2, of which 2 were waited for; matrix products, arithmetic and copies ran while one was open for 4% of the time, Pallas kernels for 0%

profile of v1, /device:TPU:1, one launch (start us, length us, event | category | flops | bytes accessed | tf_op | source)
XLA Modules:
  0.0 302.3 jit_solution(12597458500313309577)
XLA Ops:
  6.5 0.0 all-gather.2.cloned.1.call-start
  6.5 0.7 all-gather.2.cloned.1.call-update
  7.3 0.7 convert_element_type.38
  7.9 2.1 fusion.2
  10.0 97.1 %all-gather.2.cloned.1.call-done = bf16[2048,6144]{0,1:T(8,128)(2,1)} async-done(((bf16[2048,48]{0,1:T(8,128)(2,1)}), bf16[2048,6144]{0,1:T(8,128)(2,1)}) %all-gather.2.cloned.1.call-update) | async-done | bytes 25165840 | tf_op jit(solution)/shard_map/all_gather | solution.py:59
  107.1 19.9 %fusion.10 = f32[512,6144]{1,0:T(8,128)} fusion(bf16[2048,6144]{0,1:T(8,128)(2,1)} %all-gather.2.cloned.1.call-done, bf16[1,512,2048]{2,1,0:T(8,128)(2,1)} %param.5, f32[2048]{0:T(1024)S(1)} %convert_element_type.38, f32[512]{0:T(512)S(1)} %add_rsqrt_fusion.1), kind=kOutput, calls=%fused_computation.19 | convolution fusion | flops 12889096192 | bytes 39856128 | tf_op jit(solution)/shard_map/dot_general | solution.py:57
  127.0 5.7 %fusion.9 = (bf16[64,16,8,128]{3,2,1,0:T(8,128)(2,1)}, bf16[512,2048]{1,0:T(8,128)(2,1)}) fusion(f32[512,6144]{1,0:T(8,128)} %fusion.10), kind=kLoop, calls=%fused_computation.18 | loop fusion | flops 10485760 | bytes 12582912
  132.8 3.8 %slice.21 = bf16[512,2048]{1,0:T(8,128)(2,1)} slice(f32[512,6144]{1,0:T(8,128)} %fusion.10), slice={[0:512], [4096:6144]} | slice | bytes 4194304 | tf_op jit(solution)/shard_map/slice | solution.py:64
  136.6 2.9 copy.16
  139.5 4.0 %copy.17 = bf16[512,2048]{0,1:T(8,128)(2,1)} copy(bf16[512,2048]{1,0:T(8,128)(2,1)} %slice.21) | data formatting | bytes 4194304 | tf_op jit(solution)/shard_map/reshape | solution.py:64
  143.4 2.3 convolution_convert_fusion
  145.7 5.4 %stack.3 = bf16[16,1,16,128,128]{4,3,2,1,0:T(8,128)(2,1)} broadcast(bf16[16,128,128]{2,1,0:T(8,128)(2,1)S(1)} %convolution_convert_fusion), dimensions={2,3,4} | broadcast | bytes 8912896 | tf_op jit(solution)/shard_map/stack | solution.py:12
  151.2 0.0 copy-start.3
  151.2 6.7 %all-to-all-start = ((bf16[16,1,16,128,128]{4,3,2,1,0:T(8,128)(2,1)}), bf16[16,1,16,128,128]{4,3,2,1,0:T(8,128)(2,1)}, u32[]{:S(2)}, u32[]{:S(2)}) async-start(bf16[16,1,16,128,128]{4,3,2,1,0:T(8,128)(2,1)} %stack.3), calls=%async_computation | async-start | bytes 16777216 | tf_op jit(solution)/shard_map/all_to_all | solution.py:12
  157.9 0.1 iota_compare_fusion
  158.0 0.0 copy-done.3
  158.0 9.2 %fusion.8 = f32[16,128,512]{2,1,0:T(8,128)} fusion(bf16[512,16,128]{0,2,1:T(8,128)(2,1)} %bitcast.55, bf16[512,16,128]{0,2,1:T(8,128)(2,1)S(1)} %bitcast.53, pred[512,512]{1,0:T(8,128)(4,1)S(1)} %iota_compare_fusion, bf16[64,16,8,128]{3,2,1,0:T(8,128)(2,1)} %get-tuple-element.19), kind=kOutput, calls=%fused_computation.16 | convolution fusion | flops 2155872256 | bytes 10747904 | tf_op jit(solution)/shard_map/while/body/eval_jaxpr/hbc,che->bhe/dot_general | solution.py:35
  167.2 115.6 %all-to-all-done = bf16[16,1,16,128,128]{4,3,2,1,0:T(8,128)(2,1)} async-done(((bf16[16,1,16,128,128]{4,3,2,1,0:T(8,128)(2,1)}), bf16[16,1,16,128,128]{4,3,2,1,0:T(8,128)(2,1)}, u32[]{:S(2)}, u32[]{:S(2)}) %all-to-all-start) | async-done | bytes 8388640 | tf_op jit(solution)/shard_map/all_to_all | solution.py:12
  282.9 0.0 copy-start
  282.9 0.0 copy-start.1
  282.9 0.0 copy-start.2
  282.9 8.4 %fusion = f32[1,16,128,128]{3,0,2,1:T(1,128)S(1)} fusion(bf16[16,16,128,128]{3,2,1,0:T(8,128)(2,1)} %bitcast.6, s32[]{:T(128)S(6)} %axis_index.12), kind=kOutput, calls=%fused_computation.1 | convolution fusion | flops 8388624 | bytes 9437188 | tf_op jit(solution)/shard_map/c,chde->hde/dot_general | solution.py:71
  291.3 0.0 copy-done
  291.3 0.0 copy-done.1
  291.3 0.0 copy-done.2
  291.3 1.0 fusion.5
  292.4 0.6 fusion.7
  293.0 2.4 copy.11
  (3 shorter events, 0.0 us)
Async XLA Ops:
  6.5 100.6 %all-gather.2.cloned.1.call-start = ((), (), s32[]{:S(2)}) async-start(), calls=%async_computation.1 | async-start | bytes 25362432 | tf_op jit(solution)/shard_map/all_gather | solution.py:59
  151.2 6.8 %copy-start.3 = (bf16[2048]{0:T(1024)(128)(2,1)S(1)}, bf16[2048]{0:T(1024)(128)(2,1)}, u32[]{:S(2)}) copy-start(bf16[2048]{0:T(1024)(128)(2,1)} %param.8) | copy-start | bytes 12292
  151.2 131.7 %all-to-all-start = ((bf16[16,1,16,128,128]{4,3,2,1,0:T(8,128)(2,1)}), bf16[16,1,16,128,128]{4,3,2,1,0:T(8,128)(2,1)}, u32[]{:S(2)}, u32[]{:S(2)}) async-start(bf16[16,1,16,128,128]{4,3,2,1,0:T(8,128)(2,1)} %stack.3), calls=%async_computation | async-start | bytes 16777216 | tf_op jit(solution)/shard_map/all_to_all | solution.py:12
  282.9 8.5 %copy-start = (bf16[64,16,8,128]{3,2,1,0:T(8,128)(2,1)S(1)}, bf16[64,16,8,128]{3,2,1,0:T(8,128)(2,1)}, u32[]{:S(2)}) copy-start(bf16[64,16,8,128]{3,2,1,0:T(8,128)(2,1)} %get-tuple-element.19) | copy-start | bytes 6291460
  282.9 8.5 %copy-start.1 = (f32[16,128,512]{2,1,0:T(8,128)S(1)}, f32[16,128,512]{2,1,0:T(8,128)}, u32[]{:S(2)}) copy-start(f32[16,128,512]{2,1,0:T(8,128)} %fusion.8) | copy-start | bytes 12582916
  282.9 8.5 %copy-start.2 = (f32[1,16,128,128]{3,2,1,0:T(8,128)S(1)}, f32[1,16,128,128]{3,2,1,0:T(8,128)}, u32[]{:S(2)}) copy-start(f32[1,16,128,128]{3,2,1,0:T(8,128)} %param.9) | copy-start | bytes 3145732
Sparse Core Ops, SparseCore 0:
  10.4 96.6 all-gather.1
